TPU v7x, 512 devices: a whole 4x8x8 slice. The times are simulated.
512 devices in a mesh: own: 64 (over z, y), rep: 8 (over x, core).
Axes of the slice: x: 4, y: 8, z: 8, core: 2. Of those that a mesh axis runs over, the one named last changes fastest.
Arguments:
- tokens: bfloat16 [65536, 2560], P(('own', 'rep')), may hold values from -6 to 6
- cotangent: bfloat16 [65536, 2560], P(('own', 'rep')), may hold values from -6 to 6
- route: int32 [65536, 6], P(('own', 'rep')), may hold values from 0 to 159, all different within a row; in each aligned block of 128 rows (0 to 127, 128 to 255, ...) at most 6 rows name the same one
- gate_index: int32 [65536, 6], P(('own', 'rep')), may hold values from 0 to 255
- gate_table: float32 [256], replicated, may hold values from 0.1 to 1
- w_gate: bfloat16 [16384, 2560], P(('own', 'rep')), may hold values from -0.125 to 0.125
- w_up: bfloat16 [16384, 2560], P(('own', 'rep')), may hold values from -0.125 to 0.125
- w_down: bfloat16 [16384, 2560], P(('own', 'rep')), may hold values from -0.1875 to 0.1875
Outputs:
- grad_tokens: bfloat16 [65536, 2560], P(('own', 'rep'))
- grad_w_gate: float32 [16384, 2560], P(('own', 'rep'))
- grad_w_up: float32 [16384, 2560], P(('own', 'rep'))
- grad_w_down: float32 [16384, 2560], P(('own', 'rep'))
Inputs may be any that keep to these rules, and one draw needn't show every extreme that they name: `route`: each row names 6 different experts. Among the rows of one device no expert is named by more than 6 rows, and in some device some expert is named by exactly 6.
All inputs are finite; a program needn't handle non-finite values.
Results may differ from a plain program's by a relative error of at most 0.015.
Values may be sent and summed in bfloat16 or wider, within the bound.
No kernel may reach another device: no remote copies, remote signals or barrier semaphores. Data moves between devices by JAX's collectives and lax.ppermute only.
A program may use at most 64 MiB of HBM per device.

v0:
```python
import jax
import jax.numpy as jnp
from jax import lax
from jax.sharding import PartitionSpec as P

SPLIT = 4
CAP = 6


def silu_parts(pre_gate):
    sigmoid_value = jax.nn.sigmoid(pre_gate)
    return (pre_gate * sigmoid_value, sigmoid_value * (1.0 + pre_gate * (1.0 - sigmoid_value)))


def panel_terms(rows_x, rows_cot, panel_gate, panel_up, panel_down):
    pre_gate = jnp.dot(rows_x, panel_gate.T, preferred_element_type=jnp.float32)
    pre_up = jnp.dot(rows_x, panel_up.T, preferred_element_type=jnp.float32)
    active, slope_value = silu_parts(pre_gate)
    hidden = (active * pre_up).astype(jnp.bfloat16)
    hidden_delta = jnp.dot(rows_cot, panel_down.T, preferred_element_type=jnp.float32)
    gate_delta = (hidden_delta * pre_up * slope_value).astype(jnp.bfloat16)
    up_delta = (hidden_delta * active).astype(jnp.bfloat16)
    grad_rows = jnp.dot(gate_delta, panel_gate, preferred_element_type=jnp.float32) + jnp.dot(
        up_delta, panel_up, preferred_element_type=jnp.float32
    )
    grad_gate = jnp.dot(gate_delta.T, rows_x, preferred_element_type=jnp.float32)
    grad_up = jnp.dot(up_delta.T, rows_x, preferred_element_type=jnp.float32)
    grad_down = jnp.dot(hidden.T, rows_cot, preferred_element_type=jnp.float32)
    return (grad_rows, grad_gate, grad_up, grad_down)


def per_device(tokens, cotangent, route, gate_index, gate_table, w_gate, w_up, w_down):
    owners = lax.axis_size("own")
    experts_here = owners // SPLIT
    tok_count = tokens.shape[0]
    model_width = tokens.shape[1]
    choices_each = route.shape[1]
    table_hits = (
        gate_index[:, :, None] == jnp.arange(gate_table.shape[0], dtype=jnp.int32)[None, None, :]
    ).astype(jnp.float32)
    gate_values = jnp.sum(table_hits * gate_table[None, None, :], axis=2).reshape(-1)
    is_named = (
        route.reshape(-1)[:, None] == jnp.arange(experts_here, dtype=jnp.int32)[None, :]
    ).astype(jnp.int32)
    earlier = jnp.cumsum(is_named, axis=0) - is_named
    slot_hits = (
        is_named[:, :, None]
        * (earlier[:, :, None] == jnp.arange(CAP, dtype=jnp.int32)[None, None, :]).astype(jnp.int32)
    ).astype(jnp.float32)
    slot_hits = slot_hits.reshape(tok_count * choices_each, experts_here * CAP)
    select = slot_hits.reshape(tok_count, choices_each, experts_here * CAP).sum(axis=1)
    slot_gate = jnp.dot(
        gate_values, slot_hits, precision=lax.Precision.HIGHEST, preferred_element_type=jnp.float32
    )
    picker = select.astype(jnp.bfloat16)
    sent_x = jnp.dot(picker.T, tokens, preferred_element_type=jnp.float32).astype(jnp.bfloat16)
    sent_dy = jnp.dot(picker.T, cotangent, preferred_element_type=jnp.float32)
    sent_cot = (slot_gate[:, None] * sent_dy).astype(jnp.bfloat16)

    def fan_out(slot_rows):
        spread = jnp.broadcast_to(
            slot_rows.reshape(experts_here, 1, CAP, model_width),
            (experts_here, SPLIT, CAP, model_width),
        )
        return spread.reshape(owners, CAP, model_width)

    got_x, got_cot = (
        lax.all_to_all(fan_out(sent_x), "own", split_axis=0, concat_axis=0, tiled=True),
        lax.all_to_all(fan_out(sent_cot), "own", split_axis=0, concat_axis=0, tiled=True),
    )
    rows_x = got_x.reshape(owners * CAP, model_width)
    rows_cot = got_cot.reshape(owners * CAP, model_width)
    full_gate, full_up, full_down = (
        lax.all_gather(w_gate, "rep", axis=0, tiled=True),
        lax.all_gather(w_up, "rep", axis=0, tiled=True),
        lax.all_gather(w_down, "rep", axis=0, tiled=True),
    )
    grad_rows, grad_gate, grad_up, grad_down = panel_terms(
        rows_x, rows_cot, full_gate, full_up, full_down
    )
    block_rows = grad_rows.astype(jnp.bfloat16).reshape(owners, CAP, model_width)
    returned = lax.all_to_all(block_rows, "own", split_axis=0, concat_axis=0, tiled=True)
    per_slot = (
        returned.astype(jnp.float32)
        .reshape(experts_here, SPLIT, CAP, model_width)
        .sum(axis=1)
        .reshape(experts_here * CAP, model_width)
    )
    grad_tokens = jnp.dot(
        select, per_slot, precision=lax.Precision.HIGHEST, preferred_element_type=jnp.float32
    ).astype(jnp.bfloat16)
    stacked = jnp.stack([grad_gate, grad_up, grad_down]).astype(jnp.bfloat16).astype(jnp.float32)
    totals_all = lax.psum(stacked.astype(jnp.bfloat16), "rep").astype(jnp.float32)
    rows_each = stacked.shape[1] // lax.axis_size("rep")
    shares = lax.dynamic_slice_in_dim(totals_all, lax.axis_index("rep") * rows_each, rows_each, 1)
    return (grad_tokens, shares[0], shares[1], shares[2])


def solution(mesh):
    return jax.shard_map(
        per_device,
        mesh=mesh,
        in_specs=(
            P(("own", "rep"), None),
            P(("own", "rep"), None),
            P(("own", "rep"), None),
            P(("own", "rep"), None),
            P(),
            P(("own", "rep"), None),
            P(("own", "rep"), None),
            P(("own", "rep"), None),
        ),
        out_specs=(
            P(("own", "rep"), None),
            P(("own", "rep"), None),
            P(("own", "rep"), None),
            P(("own", "rep"), None),
        ),
        check_vma=False,
    )
```

profile of v0, /device:TPU:8, one launch (start us, length us, event | category | flops | bytes accessed | tf_op | source)
XLA Modules:
  0.0 346.3 jit_solution(16061698377593412336)
XLA Ops:
  7.2 0.0 copy-start
  7.2 0.9 copy.23
  8.0 0.1 eq.74
  8.2 0.1 eq.78
  8.3 1.7 reduce-window.6
  10.0 0.3 slice_reduce_fusion
  10.3 0.1 fusion.7
  10.5 8.2 %eq.83 = s32[128,6,96]{1,0,2:T(8,128)} reshape(s32[768,16,6]{0,2,1:T(8,128)S(1)} %eq.82) | data formatting | bytes 589824 | tf_op jit(solution)/shard_map/eq | solution.py:48
  18.7 0.1 select_convert_fusion
  18.8 0.0 copy-start.6
  18.8 0.0 copy-start.7
  18.8 8.2 %mul.53 = s32[128,6,96]{1,0,2:T(8,128)} reshape(s32[768,16,6]{0,2,1:T(8,128)S(1)} %mul.52) | data formatting | bytes 589824 | tf_op jit(solution)/shard_map/mul | solution.py:47
  27.0 0.1 eq.85
  27.2 0.3 select_reduce_fusion
  27.5 0.1 copy.26
  27.6 0.1 reshape.136
  27.8 0.3 convolution_bitcast_fusion
  28.1 6.5 %convert_reduce_fusion = f32[128,96]{0,1:T(8,128)S(1)} fusion(s32[128,6,96]{1,0,2:T(8,128)} %mul.53, s32[128,6,96]{1,0,2:T(8,128)} %eq.83, s32[96]{0:T(128)S(1)} %eq.85), kind=kLoop, calls=%fused_computation | loop fusion | flops 282624 | bytes 639360 | tf_op jit(solution)/shard_map/reduce_sum | solution.py:51
  34.6 0.3 fusion.4
  34.8 0.2 broadcast_in_dim.8
  35.0 1.7 broadcast_in_dim.9
  36.7 16.6 %all-to-all-start = ((bf16[64,6,2560]{2,1,0:T(8,128)(2,1)}), bf16[64,6,2560]{2,1,0:T(8,128)(2,1)S(1)}, u32[]{:S(2)}, u32[]{:S(2)}) async-start(bf16[64,6,2560]{2,1,0:T(8,128)(2,1)} %bitcast.58), calls=%async_computation | async-start | bytes 5242880 | tf_op jit(solution)/shard_map/all_to_all | solution.py:69
  53.3 0.0 all-gather.6.cloned.1.call-start
  53.4 0.7 all-gather.6.cloned.1.call-update
  54.1 0.0 all-gather.8.cloned.1.call-start
  54.1 0.7 all-gather.8.cloned.1.call-update
  54.8 2.2 convolution_convert_fusion.4
  57.0 2.0 broadcast_in_dim.10
  59.0 59.7 %all-to-all-done = bf16[64,6,2560]{2,1,0:T(8,128)(2,1)S(1)} async-done(((bf16[64,6,2560]{2,1,0:T(8,128)(2,1)}), bf16[64,6,2560]{2,1,0:T(8,128)(2,1)S(1)}, u32[]{:S(2)}, u32[]{:S(2)}) %all-to-all-start) | async-done | bytes 1966112 | tf_op jit(solution)/shard_map/all_to_all | solution.py:69
  118.7 2.8 broadcast_in_dim.11
  121.5 19.6 %all-to-all-start.1 = ((bf16[64,6,2560]{2,1,0:T(8,128)(2,1)}), bf16[64,6,2560]{2,1,0:T(8,128)(2,1)}, u32[]{:S(2)}, u32[]{:S(2)}) async-start(bf16[64,6,2560]{2,1,0:T(8,128)(2,1)} %bitcast.59), calls=%async_computation.1 | async-start | bytes 5242880 | tf_op jit(solution)/shard_map/all_to_all | solution.py:68
  141.1 0.2 all-gather.4.cloned.1.call-start
  141.3 0.5 all-gather.4.cloned.1.call-update
  141.8 2.1 reshape.127
  143.9 60.3 %all-to-all-done.1 = bf16[64,6,2560]{2,1,0:T(8,128)(2,1)} async-done(((bf16[64,6,2560]{2,1,0:T(8,128)(2,1)}), bf16[64,6,2560]{2,1,0:T(8,128)(2,1)}, u32[]{:S(2)}, u32[]{:S(2)}) %all-to-all-start.1) | async-done | bytes 1966112 | tf_op jit(solution)/shard_map/all_to_all | solution.py:68
  204.3 2.8 reshape.129
  207.0 0.0 all-gather.6.cloned.1.call-done
  207.1 2.0 fusion.13
  209.1 0.0 all-gather.8.cloned.1.call-done
  209.1 2.8 fusion.14
  211.9 2.7 multiply_convert_fusion.1
  214.6 1.9 fusion.1
  216.5 0.7 fusion.15
  217.2 0.6 copy-done.3
  217.9 2.0 fusion
  219.9 4.1 %reshape.130 = bf16[64,6,2560]{2,1,0:T(8,128)(2,1)} reshape(bf16[384,2560]{1,0:T(8,128)(2,1)} %fusion) | data formatting | bytes 3932160 | tf_op jit(solution)/shard_map/reshape | solution.py:81
  224.0 19.7 %all-to-all-start.2 = ((bf16[64,6,2560]{2,1,0:T(8,128)(2,1)}), bf16[64,6,2560]{2,1,0:T(8,128)(2,1)}, u32[]{:S(2)}, u32[]{:S(2)}) async-start(bf16[64,6,2560]{2,1,0:T(8,128)(2,1)} %reshape.130), calls=%async_computation.2 | async-start | bytes 5242880 | tf_op jit(solution)/shard_map/all_to_all | solution.py:82
  243.7 0.0 all-reduce.2.cloned.1.call-start
  243.8 0.0 copy-start.1
  243.8 0.0 copy-start.5
  243.8 0.9 fusion.2
  244.7 0.7 copy-done.1
  245.3 0.0 copy-done.5
  245.4 0.9 fusion.3
  246.3 0.4 copy-done.2
  246.7 2.1 pad_maximum_fusion
  248.8 0.0 all-reduce.2.cloned.1.call-update
  248.8 84.3 %all-reduce.2.cloned.1.call-done = bf16[3,256,2560]{2,1,0:T(8,128)(2,1)} async-done(((bf16[3,256,2560]{2,1,0:T(8,128)(2,1)}), bf16[3,256,2560]{2,1,0:T(8,128)(2,1)}) %all-reduce.2.cloned.1.call-update) | async-done | bytes 3932176 | tf_op jit(solution)/shard_map/psum | solution.py:93
  333.1 1.1 dynamic-slice_convert_fusion
  334.2 1.0 slice_bitcast_fusion
  335.2 0.0 all-to-all-done.2
  335.2 2.4 convert_reduce_fusion.1
  337.6 0.1 reshape.133
  337.7 2.1 convolution_convert_fusion.3
  (15 shorter events, 0.2 us)
Async XLA Ops:
  7.2 27.4 %copy-start = (bf16[128,2560]{1,0:T(8,128)(2,1)S(1)}, bf16[128,2560]{1,0:T(8,128)(2,1)}, u32[]{:S(2)}) copy-start(bf16[128,2560]{1,0:T(8,128)(2,1)} %param.9) | copy-start | bytes 1966084
  18.8 8.4 %copy-start.6 = (s32[128,6]{0,1:T(8,128)S(1)}, s32[128,6]{0,1:T(8,128)}, u32[]{:S(2)}) copy-start(s32[128,6]{0,1:T(8,128)} %param.11) | copy-start | bytes 9220
  18.8 8.4 %copy-start.7 = (f32[256]{0:T(256)S(1)}, f32[256]{0:T(256)}, u32[]{:S(2)}) copy-start(f32[256]{0:T(256)} %param.12) | copy-start | bytes 3076
  36.7 81.9 %all-to-all-start = ((bf16[64,6,2560]{2,1,0:T(8,128)(2,1)}), bf16[64,6,2560]{2,1,0:T(8,128)(2,1)S(1)}, u32[]{:S(2)}, u32[]{:S(2)}) async-start(bf16[64,6,2560]{2,1,0:T(8,128)(2,1)} %bitcast.58), calls=%async_computation | async-start | bytes 5242880 | tf_op jit(solution)/shard_map/all_to_all | solution.py:69
  53.3 153.7 %all-gather.6.cloned.1.call-start = ((), (), s32[]{:S(2)}) async-start(), calls=%async_computation.4 | async-start | bytes 1474560 | tf_op jit(solution)/shard_map/all_gather | solution.py:75
  54.1 155.0 %all-gather.8.cloned.1.call-start = ((), (), s32[]{:S(2)}) async-start(), calls=%async_computation.5 | async-start | bytes 1474560 | tf_op jit(solution)/shard_map/all_gather | solution.py:74
  121.5 82.8 %all-to-all-start.1 = ((bf16[64,6,2560]{2,1,0:T(8,128)(2,1)}), bf16[64,6,2560]{2,1,0:T(8,128)(2,1)}, u32[]{:S(2)}, u32[]{:S(2)}) async-start(bf16[64,6,2560]{2,1,0:T(8,128)(2,1)} %bitcast.59), calls=%async_computation.1 | async-start | bytes 5242880 | tf_op jit(solution)/shard_map/all_to_all | solution.py:68
  141.1 70.8 %all-gather.4.cloned.1.call-start = ((), (), s32[]{:S(2)}) async-start(), calls=%async_computation.3 | async-start | bytes 1474560 | tf_op jit(solution)/shard_map/all_gather | solution.py:76
  214.6 1.9 copy-start.4
  216.5 1.3 copy-start.3
  224.0 111.1 %all-to-all-start.2 = ((bf16[64,6,2560]{2,1,0:T(8,128)(2,1)}), bf16[64,6,2560]{2,1,0:T(8,128)(2,1)}, u32[]{:S(2)}, u32[]{:S(2)}) async-start(bf16[64,6,2560]{2,1,0:T(8,128)(2,1)} %reshape.130), calls=%async_computation.2 | async-start | bytes 5242880 | tf_op jit(solution)/shard_map/all_to_all | solution.py:82
  243.7 89.3 %all-reduce.2.cloned.1.call-start = ((), (), s32[]{:S(2)}) async-start(), calls=%async_computation.6 | async-start | bytes 7864320 | tf_op jit(solution)/shard_map/psum | solution.py:93
  243.8 1.5 copy-start.1
  243.8 1.6 copy-start.5
  245.4 1.3 copy-start.2
Sparse Core Ops, SparseCore 0:
  56.3 29.6 all-gather.5
  88.1 29.1 all-gather.7
  144.0 29.4 all-gather.3
  248.9 84.0 all-reduce.1
where the time goes:
time: 347 us; the launch traced here: 346 us
  waiting for transfers between devices  206 us (59%)
  starting transfers between devices  56.2 us (16%)
  local copies, waits for them, and re-layouts  36.9 us (11%)
  matrix products  18.7 us (5%)
  other arithmetic  14.3 us (4%)
  between operations  14 us (4%)
    psum x1, waiting for transfers between devices, per_device(): lax.psum(stacked.astype(jnp.bfloat16), 'rep').astype(jnp.float32)  84.3 us
    all_to_all x1, waiting for transfers between devices, per_device(): lax.all_to_all(fan_out(sent_x), 'own', split_axis=0, concat_axis=0, tiled...  60.3 us
    all_to_all x1, waiting for transfers between devices, per_device(): lax.all_to_all(fan_out(sent_cot), 'own', split_axis=0, concat_axis=0, til...  59.7 us
    all_to_all x1, starting transfers between devices, per_device(): lax.all_to_all(block_rows, 'own', split_axis=0, concat_axis=0, tiled=True)  19.7 us
    all_to_all x1, starting transfers between devices, per_device(): lax.all_to_all(fan_out(sent_x), 'own', split_axis=0, concat_axis=0, tiled...  19.6 us
    all_to_all x1, starting transfers between devices, per_device(): lax.all_to_all(fan_out(sent_cot), 'own', split_axis=0, concat_axis=0, til...  16.6 us
    eq x4, local copies, waits for them, and re-layouts, per_device(): earlier[:, :, None] == jnp.arange(CAP, dtype=jnp.int32)[None, None, :]  8.34 us
    mul x2, local copies, waits for them, and re-layouts, per_device(): is_named[:, :, None]  8.27 us
  transfers between devices with their start and end apart: 7, of which 3 were waited for; matrix products, arithmetic and copies ran while one was open for 7% of the time, Pallas kernels for 0%

commit v1 on v0

--- a/solution.py
+++ b/solution.py
@@ -5,6 +5,7 @@
 
 SPLIT = 4
 CAP = 6
+work_patches = lambda patch, named_axis: lax.all_gather(patch, axis_name=named_axis).sum(axis=0)
 
 
 def silu_parts(pre_gate):
@@ -90,7 +91,7 @@
         select, per_slot, precision=lax.Precision.HIGHEST, preferred_element_type=jnp.float32
     ).astype(jnp.bfloat16)
     stacked = jnp.stack([grad_gate, grad_up, grad_down]).astype(jnp.bfloat16).astype(jnp.float32)
-    totals_all = lax.psum(stacked.astype(jnp.bfloat16), "rep").astype(jnp.float32)
+    totals_all = work_patches(stacked.astype(jnp.bfloat16), "rep").astype(jnp.float32)
     rows_each = stacked.shape[1] // lax.axis_size("rep")
     shares = lax.dynamic_slice_in_dim(totals_all, lax.axis_index("rep") * rows_each, rows_each, 1)
     return (grad_tokens, shares[0], shares[1], shares[2])

time: 347 us -> 405 us (1.17)
  the two profiles are of different devices: /device:TPU:8 before, /device:TPU:1 now
where the time goes in v1:
time: 405 us; the launch traced here: 404 us
  waiting for transfers between devices  247 us (61%)
  starting transfers between devices  59.2 us (15%)
  local copies, waits for them, and re-layouts  38.5 us (10%)
  other arithmetic  27 us (7%)
  matrix products  17.8 us (4%)
  between operations  14 us (3%)
    all_gather x1, waiting for transfers between devices, lax.all_gather(patch, axis_name=named_axis).sum(axis=0)  70.2 us
    all_to_all x1, waiting for transfers between devices, per_device(): lax.all_to_all(block_rows, 'own', split_axis=0, concat_axis=0, tiled=True)  61.5 us
    all_to_all x1, waiting for transfers between devices, per_device(): lax.all_to_all(fan_out(sent_cot), 'own', split_axis=0, concat_axis=0, til...  58.3 us
    all_to_all x1, waiting for transfers between devices, per_device(): lax.all_to_all(fan_out(sent_x), 'own', split_axis=0, concat_axis=0, tiled...  55 us
    all_to_all x1, starting transfers between devices, per_device(): lax.all_to_all(fan_out(sent_cot), 'own', split_axis=0, concat_axis=0, til...  22.2 us
    all_to_all x1, starting transfers between devices, per_device(): lax.all_to_all(block_rows, 'own', split_axis=0, concat_axis=0, tiled=True)  19.4 us
    all_to_all x1, starting transfers between devices, per_device(): lax.all_to_all(fan_out(sent_x), 'own', split_axis=0, concat_axis=0, tiled...  17.3 us
    reduce_sum x1, other arithmetic, lax.all_gather(patch, axis_name=named_axis).sum(axis=0)  13.6 us
  transfers between devices with their start and end apart: 7, of which 4 were waited for; matrix products, arithmetic and copies ran while one was open for 7% of the time, Pallas kernels for 0%

profile of v1, /device:TPU:1, one launch (start us, length us, event | category | flops | bytes accessed | tf_op | source)
XLA Modules:
  0.0 403.7 jit_solution(7479179454041629437)
XLA Ops:
  7.2 0.0 copy-start
  7.2 0.9 copy.23
  8.0 0.1 eq.78
  8.2 0.1 eq.74
  8.4 8.3 %mul.53 = s32[128,6,96]{1,0,2:T(8,128)} reshape(s32[768,16,6]{0,2,1:T(8,128)S(1)} %mul.52) | data formatting | bytes 589824 | tf_op jit(solution)/shard_map/mul | solution.py:48
  16.6 1.7 reduce-window.6
  18.3 0.3 slice_reduce_fusion
  18.6 0.1 fusion.7
  18.8 8.2 %eq.83 = s32[128,6,96]{1,0,2:T(8,128)} reshape(s32[768,16,6]{0,2,1:T(8,128)S(1)} %eq.82) | data formatting | bytes 589824 | tf_op jit(solution)/shard_map/eq | solution.py:49
  27.0 0.1 eq.85
  27.1 6.4 %convert_reduce_fusion = f32[128,96]{0,1:T(8,128)S(1)} fusion(s32[128,6,96]{1,0,2:T(8,128)} %mul.53, s32[128,6,96]{1,0,2:T(8,128)} %eq.83, s32[96]{0:T(128)S(1)} %eq.85), kind=kLoop, calls=%fused_computation | loop fusion | flops 282624 | bytes 639360 | tf_op jit(solution)/shard_map/reduce_sum | solution.py:52
  33.5 0.0 copy-done
  33.5 0.3 convolution_convert_fusion.4
  33.8 0.2 broadcast_in_dim.10
  34.0 1.7 broadcast_in_dim.11
  35.7 17.3 %all-to-all-start.1 = ((bf16[64,6,2560]{2,1,0:T(8,128)(2,1)}), bf16[64,6,2560]{2,1,0:T(8,128)(2,1)S(1)}, u32[]{:S(2)}, u32[]{:S(2)}) async-start(bf16[64,6,2560]{2,1,0:T(8,128)(2,1)} %bitcast.58), calls=%async_computation.1 | async-start | bytes 5242880 | tf_op jit(solution)/shard_map/all_to_all | solution.py:69
  52.9 0.0 all-gather.9.cloned.1.call-start
  53.0 0.7 all-gather.9.cloned.1.call-update
  53.7 0.3 select_reduce_fusion
  54.0 0.1 copy.26
  54.1 0.1 reshape.184
  54.3 0.1 select_convert_fusion
  54.3 0.8 convert_element_type.73
  55.1 1.3 convolution_bitcast_fusion
  56.4 2.2 fusion.4
  58.6 1.2 broadcast_in_dim.8
  59.8 55.0 %all-to-all-done.1 = bf16[64,6,2560]{2,1,0:T(8,128)(2,1)S(1)} async-done(((bf16[64,6,2560]{2,1,0:T(8,128)(2,1)}), bf16[64,6,2560]{2,1,0:T(8,128)(2,1)S(1)}, u32[]{:S(2)}, u32[]{:S(2)}) %all-to-all-start.1) | async-done | bytes 1966112 | tf_op jit(solution)/shard_map/all_to_all | solution.py:69
  114.8 1.8 broadcast_in_dim.9
  116.6 0.4 copy-done.2
  117.1 22.2 %all-to-all-start = ((bf16[64,6,2560]{2,1,0:T(8,128)(2,1)}), bf16[64,6,2560]{2,1,0:T(8,128)(2,1)}, u32[]{:S(2)}, u32[]{:S(2)}) async-start(bf16[64,6,2560]{2,1,0:T(8,128)(2,1)} %bitcast.59), calls=%async_computation | async-start | bytes 5242880 | tf_op jit(solution)/shard_map/all_to_all | solution.py:70
  139.3 0.0 all-gather.7.cloned.1.call-start
  139.3 0.7 all-gather.7.cloned.1.call-update
  140.0 0.0 all-gather.5.cloned.1.call-start
  140.1 0.7 all-gather.5.cloned.1.call-update
  140.8 0.2 all-gather.11.cloned.1.call-start
  141.0 2.8 reshape.177
  143.8 58.3 %all-to-all-done = bf16[64,6,2560]{2,1,0:T(8,128)(2,1)} async-done(((bf16[64,6,2560]{2,1,0:T(8,128)(2,1)}), bf16[64,6,2560]{2,1,0:T(8,128)(2,1)}, u32[]{:S(2)}, u32[]{:S(2)}) %all-to-all-start) | async-done | bytes 1966112 | tf_op jit(solution)/shard_map/all_to_all | solution.py:70
  202.1 4.1 %reshape.175 = bf16[384,2560]{1,0:T(8,128)(2,1)} reshape(bf16[64,6,2560]{2,1,0:T(8,128)(2,1)} %all-to-all-done) | data formatting | bytes 3932160 | tf_op jit(solution)/shard_map/reshape | solution.py:73
  206.2 2.0 fusion.14
  208.3 0.0 all-gather.7.cloned.1.call-done
  208.3 2.2 fusion.13
  210.5 0.0 copy-start.7
  210.5 2.0 fusion.3
  212.5 2.7 multiply_convert_fusion.1
  215.2 0.9 fusion.2
  216.1 0.0 copy-start.4
  216.1 0.9 fusion.1
  217.0 0.4 copy-done.4
  217.4 2.1 pad_maximum_fusion
  219.5 0.0 all-gather.11.cloned.1.call-update
  219.5 1.3 copy-done.6
  220.8 0.7 fusion.15
  221.5 0.6 copy-done.5
  222.1 0.7 fusion
  222.8 2.3 reshape.178
  225.2 19.4 %all-to-all-start.2 = ((bf16[64,6,2560]{2,1,0:T(8,128)(2,1)}), bf16[64,6,2560]{2,1,0:T(8,128)(2,1)S(1)}, u32[]{:S(2)}, u32[]{:S(2)}) async-start(bf16[64,6,2560]{2,1,0:T(8,128)(2,1)} %reshape.178), calls=%async_computation.2 | async-start | bytes 5242880 | tf_op jit(solution)/shard_map/all_to_all | solution.py:83
  244.6 61.5 %all-to-all-done.2 = bf16[64,6,2560]{2,1,0:T(8,128)(2,1)S(1)} async-done(((bf16[64,6,2560]{2,1,0:T(8,128)(2,1)}), bf16[64,6,2560]{2,1,0:T(8,128)(2,1)S(1)}, u32[]{:S(2)}, u32[]{:S(2)}) %all-to-all-start.2) | async-done | bytes 1966112 | tf_op jit(solution)/shard_map/all_to_all | solution.py:83
  306.1 1.6 convert_reduce_fusion.1
  307.7 1.5 reshape.181
  309.2 2.1 convolution_convert_fusion.3
  311.3 70.2 %all-gather.11.cloned.1.call-done = bf16[8,3,256,2560]{3,2,1,0:T(8,128)(2,1)} async-done(((bf16[1,3,256,2560]{3,2,1,0:T(8,128)(2,1)}), bf16[8,3,256,2560]{3,2,1,0:T(8,128)(2,1)}) %all-gather.11.cloned.1.call-update) | async-done | bytes 31457296 | tf_op jit(solution)/shard_map/all_gather | solution.py:8
  381.5 13.6 %reduce_sum.42 = bf16[3,256,2560]{2,1,0:T(8,128)(2,1)} reduce(bf16[8,3,256,2560]{3,2,1,0:T(8,128)(2,1)} %all-gather.11.cloned.1.call-done, bf16[]{:T(256)} %constant.17.clone.1), dimensions={0}, to_apply=%region_5.6 | reduce | flops 13762560 | bytes 35389440 | tf_op jit(solution)/shard_map/reduce_sum | solution.py:8
  395.1 1.1 dynamic-slice_convert_fusion
  396.2 1.0 slice_bitcast_fusion
  (20 shorter events, 0.1 us)
Async XLA Ops:
  7.2 26.3 %copy-start = (bf16[128,2560]{1,0:T(8,128)(2,1)S(1)}, bf16[128,2560]{1,0:T(8,128)(2,1)}, u32[]{:S(2)}) copy-start(bf16[128,2560]{1,0:T(8,128)(2,1)} %param.8) | copy-start | bytes 1966084
  35.7 18.0 %copy-start.8 = (s32[128,6]{0,1:T(8,128)S(1)}, s32[128,6]{0,1:T(8,128)}, u32[]{:S(2)}) copy-start(s32[128,6]{0,1:T(8,128)} %param.11) | copy-start | bytes 9220
  35.7 18.0 %copy-start.9 = (f32[256]{0:T(256)S(1)}, f32[256]{0:T(256)}, u32[]{:S(2)}) copy-start(f32[256]{0:T(256)} %param.12) | copy-start | bytes 3076
  35.7 79.1 %all-to-all-start.1 = ((bf16[64,6,2560]{2,1,0:T(8,128)(2,1)}), bf16[64,6,2560]{2,1,0:T(8,128)(2,1)S(1)}, u32[]{:S(2)}, u32[]{:S(2)}) async-start(bf16[64,6,2560]{2,1,0:T(8,128)(2,1)} %bitcast.58), calls=%async_computation.1 | async-start | bytes 5242880 | tf_op jit(solution)/shard_map/all_to_all | solution.py:69
  52.9 153.3 %all-gather.9.cloned.1.call-start = ((), (), s32[]{:S(2)}) async-start(), calls=%async_computation.5 | async-start | bytes 1474560 | tf_op jit(solution)/shard_map/all_gather | solution.py:75
  114.8 2.3 copy-start.2
  117.1 85.0 %all-to-all-start = ((bf16[64,6,2560]{2,1,0:T(8,128)(2,1)}), bf16[64,6,2560]{2,1,0:T(8,128)(2,1)}, u32[]{:S(2)}, u32[]{:S(2)}) async-start(bf16[64,6,2560]{2,1,0:T(8,128)(2,1)} %bitcast.59), calls=%async_computation | async-start | bytes 5242880 | tf_op jit(solution)/shard_map/all_to_all | solution.py:70
  139.3 69.0 %all-gather.7.cloned.1.call-start = ((), (), s32[]{:S(2)}) async-start(), calls=%async_computation.4 | async-start | bytes 1474560 | tf_op jit(solution)/shard_map/all_gather | solution.py:76
  140.0 72.5 %all-gather.5.cloned.1.call-start = ((), (), s32[]{:S(2)}) async-start(), calls=%async_computation.3 | async-start | bytes 1474560 | tf_op jit(solution)/shard_map/all_gather | solution.py:77
  140.8 240.7 %all-gather.11.cloned.1.call-start = ((), (), s32[]{:S(2)}) async-start(), calls=%async_computation.6 | async-start | bytes 35389440 | tf_op jit(solution)/shard_map/all_gather | solution.py:8
  208.3 2.2 copy-start.3
  210.5 2.0 copy-start.7
  216.1 1.3 copy-start.4
  219.5 1.3 copy-start.6
  220.8 1.3 copy-start.5
  225.2 80.9 %all-to-all-start.2 = ((bf16[64,6,2560]{2,1,0:T(8,128)(2,1)}), bf16[64,6,2560]{2,1,0:T(8,128)(2,1)S(1)}, u32[]{:S(2)}, u32[]{:S(2)}) async-start(bf16[64,6,2560]{2,1,0:T(8,128)(2,1)} %reshape.178), calls=%async_computation.2 | async-start | bytes 5242880 | tf_op jit(solution)/shard_map/all_to_all | solution.py:83
  381.5 15.7 %copy-start.1 = (bf16[128,2560]{1,0:T(8,128)(2,1)S(1)}, bf16[128,2560]{1,0:T(8,128)(2,1)}, u32[]{:S(2)}) copy-start(bf16[128,2560]{1,0:T(8,128)(2,1)} %param.8) | copy-start | bytes 1966084
Sparse Core Ops, SparseCore 0:
  55.9 30.4 all-gather.8
  142.2 31.2 all-gather.6
  175.6 29.0 all-gather.4
  219.6 161.7 all-gather.10
